TPU v7x, 32 devices: a whole 2x2x4 slice. The times are simulated.
32 devices in a mesh: groups: 2 (over y), lon: 4 (over z), chan: 2 (over x), lat: 2 (over core).
Axes of the slice: x: 2, y: 2, z: 4, core: 2. Of those that a mesh axis runs over, the one named last changes fastest.
Arguments:
- inputs: bfloat16 [256, 64, 512], P('chan', ('groups', 'lat'), 'lon'), parts along dimension 1, may hold values from -6 to 6
- cotangent: bfloat16 [256, 64, 512], P('chan', ('groups', 'lat'), 'lon'), parts along dimension 1, may hold values from -6 to 6
- weight: bfloat16 [3, 3, 256, 256], P(None, None, 'chan'), may hold values from -0.125 to 0.125
- bias_vector: float32 [256], P('chan'), may hold values from -4 to 4
Outputs:
- input_grad: bfloat16 [256, 64, 512], P('chan', ('groups', 'lat'), 'lon'), parts along dimension 1
- weight_grad: float32 [6, 3, 256, 256], P('groups', None, 'chan'), parts along dimension 0
- bias_grad: float32 [512], P(('groups', 'chan')), parts along dimension 0
There are 2 independent parts, one for each index of `groups`. A program takes and returns all parts, laid end to end along the dimension named above; an argument that names none is the same for every part. Nothing has to cross between parts.
All inputs are finite; a program needn't handle non-finite values.
Results may differ from a plain program's by a relative error of at most 0.007.
Values may be sent and summed in bfloat16 or wider, within the bound.
No kernel may reach another device: no remote copies, remote signals or barrier semaphores. Data moves between devices by JAX's collectives and lax.ppermute only.
A program may use at most 64 MiB of HBM per device.

v0:
```python
import jax
import jax.numpy as jnp
from jax import lax
from jax.sharding import PartitionSpec as P


def padded_2(shard, sides, width):
    for axis, dim in sides:
        devices, length = (lax.axis_size(axis), shard.shape[dim])
        up = [(i, (i + 1) % devices) for i in range(devices)]
        down = [(j, i) for i, j in up]
        last = lax.slice_in_dim(shard, length - width, length, axis=dim)
        initial = lax.slice_in_dim(shard, 0, width, axis=dim)
        before = lax.ppermute(last, axis, up)
        after = lax.ppermute(initial, axis, down)
        shard = jnp.concatenate([before, shard, after], axis=dim)
    return shard


def gelu_slope(preact):
    normal_cdf = 0.5 * (1.0 + jax.scipy.special.erf(preact * 0.7071067811865476))
    density = jnp.exp(-0.5 * preact * preact) * 0.3989422804014327
    return normal_cdf + preact * density


def mask_rims(padded):
    lat_index = lax.axis_index("lat")
    band_count = lax.axis_size("lat")
    row_ids = jnp.arange(padded.shape[1])
    outside = (row_ids == 0) & (lat_index == 0) | (row_ids == padded.shape[1] - 1) & (
        lat_index == band_count - 1
    )
    return jnp.where(outside[None, :, None], jnp.zeros((), padded.dtype), padded)


def window_of(field, first_row, first_col, row_count, column_count):
    return field[
        :, first_row : first_row + row_count, first_col : first_col + column_count
    ].reshape(field.shape[0], -1)


def local(inputs, cotangent, weight, bias_vector):
    own_channels, row_count, column_count = inputs.shape
    input_pad = mask_rims(padded_2(inputs, (("lon", 2), ("lat", 1)), 1))
    input_all = lax.all_gather(input_pad, "chan", axis=0, tiled=True)
    preact = jnp.zeros((own_channels, row_count * column_count), jnp.float32)
    for tap_row in range(3):
        for tap_col in range(3):
            window = window_of(input_all, tap_row, tap_col, row_count, column_count)
            preact = preact + jnp.dot(
                weight[tap_row, tap_col], window, preferred_element_type=jnp.float32
            )
    preact = preact + bias_vector[:, None]
    upstream = cotangent.reshape(own_channels, -1).astype(jnp.float32)
    grad_pre = (upstream * gelu_slope(preact)).astype(jnp.bfloat16)
    bias_part = jnp.sum(grad_pre.astype(jnp.float32), axis=1)
    taps = []
    for tap_row in range(3):
        row_taps = []
        for tap_col in range(3):
            window = window_of(input_all, tap_row, tap_col, row_count, column_count)
            row_taps.append(
                lax.dot_general(
                    grad_pre, window, (((1,), (1,)), ((), ())), preferred_element_type=jnp.float32
                )
            )
        taps.append(jnp.stack(row_taps))
    weight_part = jnp.stack(taps)
    weight_grad, bias_grad = lax.psum((weight_part, bias_part), ("lon", "lat"))
    grad_field = grad_pre.reshape(own_channels, row_count, column_count)
    grad_pad = mask_rims(padded_2(grad_field, (("lon", 2), ("lat", 1)), 1))
    amount = lax.axis_size("chan") * own_channels
    summed = jnp.zeros((amount, row_count * column_count), jnp.float32)
    for tap_row in range(3):
        for tap_col in range(3):
            kernel_cols = weight[tap_row, tap_col]
            window = window_of(grad_pad, 2 - tap_row, 2 - tap_col, row_count, column_count)
            summed = summed + lax.dot_general(
                kernel_cols, window, (((0,), (0,)), ((), ())), preferred_element_type=jnp.float32
            )
    input_sum = lax.psum_scatter(
        summed.reshape(amount, row_count, column_count), "chan", scatter_dimension=0, tiled=True
    )
    return (input_sum.astype(jnp.bfloat16), weight_grad, bias_grad)


def solution(mesh):
    placed = (
        P("chan", ("groups", "lat"), "lon"),
        P("chan", ("groups", "lat"), "lon"),
        P(None, None, "chan", None),
        P("chan"),
    )
    return jax.shard_map(
        local,
        mesh=mesh,
        in_specs=placed,
        out_specs=(
            P("chan", ("groups", "lat"), "lon"),
            P("groups", None, "chan", None),
            P(("groups", "chan")),
        ),
        check_vma=False,
    )
```

profile of v0, /device:TPU:0, one launch (start us, length us, event | category | flops | bytes accessed | tf_op | source)
XLA Modules:
  0.0 177.4 jit_solution(9235394544272731963)
XLA Ops:
  7.2 1.5 copy.13
  8.8 3.1 %collective-permute-start = (bf16[128,16,1]{0,2,1:T(2,128)(2,1)S(1)}, bf16[128,16,1]{0,2,1:T(2,128)(2,1)S(1)}, u32[]{:S(2)}, u32[]{:S(2)}) collective-permute-start(bf16[128,16,1]{0,2,1:T(2,128)(2,1)S(1)} %get-tuple-element.27), channel_id=1, source_target_pairs={{0,4},{4,8},{8,12},{12,0},{1,5},{5,9},{9,13},{13,1},{2,6},{6,10},{... | collective-permute-start | bytes 12296 | tf_op jit(solution)/shard_map/ppermute | solution.py:14
  11.8 2.1 %collective-permute-start.1 = (bf16[128,16,1]{0,2,1:T(2,128)(2,1)S(1)}, bf16[128,16,1]{0,2,1:T(2,128)(2,1)S(1)}, u32[]{:S(2)}, u32[]{:S(2)}) collective-permute-start(bf16[128,16,1]{0,2,1:T(2,128)(2,1)S(1)} %get-tuple-element.28), channel_id=1, source_target_pairs={{4,0},{8,4},{12,8},{0,12},{5,1},{9,5},{13,9},{1,13},{6,2},{10,6},{... | collective-permute-start | bytes 12296 | tf_op jit(solution)/shard_map/ppermute | solution.py:15
  13.9 1.6 collective-permute-done
  15.7 0.5 collective-permute-start.3
  16.2 0.7 collective-permute-done.2
  17.0 1.1 maximum_select_fusion
  18.2 1.4 copy.12
  19.6 23.9 %all-gather.2.cloned.1.call-done = bf16[256,18,130]{0,2,1:T(8,128)(2,1)} async-done(((bf16[128,18,130]{0,2,1:T(8,128)(2,1)}), bf16[256,18,130]{0,2,1:T(8,128)(2,1)}) %all-gather.2.cloned.1.call-update) | async-done | bytes 1198096 | tf_op jit(solution)/shard_map/all_gather | solution.py:45
  43.5 8.3 %fusion.46 = (bf16[256,16,128]{0,2,1:T(8,128)(2,1)S(1)}, bf16[256,16,128]{0,2,1:T(8,128)(2,1)S(1)}, bf16[256,16,128]{0,2,1:T(8,128)(2,1)S(1)}, bf16[256,16,128]{...) fusion(bf16[256,18,130]{0,2,1:T(8,128)(2,1)} %all-gather.2.clon, ...), kind=kLoop, calls=%fused_computation.86 | loop fusion | bytes 18874368 | tf_op jit(solution)/shard_map/slice | solution.py:37
  52.3 0.4 convolution_add_fusion.15
  54.6 0.4 convolution_add_fusion.10
  55.6 0.7 copy-done.13
  56.3 0.7 convert_reduce_fusion
  57.1 1.5 collective-permute-start.4
  58.6 2.3 %collective-permute-start.5 = (bf16[128,16,1]{0,2,1:T(2,128)(2,1)S(1)}, bf16[128,16,1]{0,2,1:T(2,128)(2,1)S(1)}, u32[]{:S(2)}, u32[]{:S(2)}) collective-permute-start(bf16[128,16,1]{0,2,1:T(2,128)(2,1)S(1)} %get-tuple-element.26), channel_id=1, source_target_pairs={{4,0},{8,4},{12,8},{0,12},{5,1},{9,5},{13,9},{1,13},{6,2},{10,6},{... | collective-permute-start | bytes 12296 | tf_op jit(solution)/shard_map/ppermute | solution.py:15
  60.9 1.6 collective-permute-done.4
  62.7 0.5 collective-permute-start.7
  63.2 0.7 collective-permute-done.6
  64.4 0.9 fusion.47
  68.6 1.7 convolution_add_fusion
  70.4 3.0 %copy.16 = f32[256,16,128]{2,1,0:T(8,128)} copy(f32[256,16,128]{0,2,1:T(8,128)} %bitcast.154) | data formatting | bytes 4194304 | tf_op jit(solution)/shard_map/reshape | solution.py:82
  73.6 1.7 convolution_bitcast_fusion
  75.3 1.7 convolution_bitcast_fusion.1
  77.8 0.4 copy-done.5
  79.0 0.5 copy-done.1
  80.6 1.1 pad_maximum_fusion
  81.8 17.9 %psum.15 = f32[128]{0:T(128)} all-reduce(f32[128]{0:T(128)S(1)} %get-tuple-element.29), channel_id=1, replica_groups=mesh['groups'=2,'lon'=4,'chan'=2,'lat'=2] {'lon','lat'}, use_global_device_ids=true, to_apply=%region_3.4 | all-reduce | flops 128 | bytes 1024 | tf_op jit(solution)/shard_map/psum | solution.py:69
  99.6 6.3 %reduce-scatter.2.cloned.1.call-done = f32[128,16,128]{2,1,0:T(8,128)} async-done(((f32[256,16,128]{2,1,0:T(8,128)}), f32[128,16,128]{2,1,0:T(8,128)}) %reduce-scatter.2.cloned.1.call-update) | async-done | bytes 1048592 | tf_op jit(solution)/shard_map/reduce_scatter | solution.py:81
  105.9 2.1 %convert_element_type.18 = bf16[128,16,128]{2,1,0:T(8,128)(2,1)} convert(f32[128,16,128]{2,1,0:T(8,128)} %reduce-scatter.2.cloned.1.call-done) | non-fusion elementwise | flops 262144 | bytes 1572864 | tf_op jit(solution)/shard_map/convert_element_type | solution.py:84
  108.0 60.5 %all-reduce.2.cloned.1.call-done = f32[3,3,128,256]{3,2,1,0:T(8,128)} async-done(((f32[3,3,128,256]{3,2,1,0:T(8,128)}), f32[3,3,128,256]{3,2,1,0:T(8,128)}) %all-reduce.2.cloned.1.call-update) | async-done | bytes 1179664 | tf_op jit(solution)/shard_map/psum | solution.py:69
  168.5 2.4 %copy.18 = f32[3,3,128,256]{3,2,1,0:T(8,128)} copy(f32[3,3,128,256]{3,2,1,0:T(8,128)} %all-reduce.2.cloned.1.call-done) | data formatting | bytes 2359296
  (70 shorter events, 9.9 us)
Async XLA Ops:
  7.2 11.1 %copy-start.14 = (bf16[128,16,128]{2,1,0:T(8,128)(2,1)S(1)}, bf16[128,16,128]{2,1,0:T(8,128)(2,1)}, u32[]{:S(2)}) copy-start(bf16[128,16,128]{2,1,0:T(8,128)(2,1)} %param.5) | copy-start | bytes 1572868
  7.2 36.3 %all-gather.2.cloned.1.call-start = ((), (), s32[]{:S(2)}) async-start(), calls=%async_computation.1 | async-start | bytes 1880064 | tf_op jit(solution)/shard_map/all_gather | solution.py:45
  8.8 6.8 %collective-permute-start = (bf16[128,16,1]{0,2,1:T(2,128)(2,1)S(1)}, bf16[128,16,1]{0,2,1:T(2,128)(2,1)S(1)}, u32[]{:S(2)}, u32[]{:S(2)}) collective-permute-start(bf16[128,16,1]{0,2,1:T(2,128)(2,1)S(1)} %get-tuple-element.27), channel_id=1, source_target_pairs={{0,4},{4,8},{8,12},{12,0},{1,5},{5,9},{9,13},{13,1},{2,6},{6,10},{... | collective-permute-start | bytes 12296 | tf_op jit(solution)/shard_map/ppermute | solution.py:14
  11.8 3.7 %collective-permute-start.1 = (bf16[128,16,1]{0,2,1:T(2,128)(2,1)S(1)}, bf16[128,16,1]{0,2,1:T(2,128)(2,1)S(1)}, u32[]{:S(2)}, u32[]{:S(2)}) collective-permute-start(bf16[128,16,1]{0,2,1:T(2,128)(2,1)S(1)} %get-tuple-element.28), channel_id=1, source_target_pairs={{4,0},{8,4},{12,8},{0,12},{5,1},{9,5},{13,9},{1,13},{6,2},{10,6},{... | collective-permute-start | bytes 12296 | tf_op jit(solution)/shard_map/ppermute | solution.py:15
  15.6 1.3 collective-permute-start.2
  15.7 1.4 collective-permute-start.3
  18.2 87.8 %reduce-scatter.2.cloned.1.call-start = ((), (), s32[]{:S(2)}) async-start(), calls=%async_computation.2 | async-start | bytes 3145728 | tf_op jit(solution)/shard_map/reduce_scatter | solution.py:81
  19.6 32.3 %copy-start.12 = (bf16[3,3,128,256]{3,2,1,0:T(8,128)(2,1)S(1)}, bf16[3,3,128,256]{3,2,1,0:T(8,128)(2,1)}, u32[]{:S(2)}) copy-start(bf16[3,3,128,256]{3,2,1,0:T(8,128)(2,1)} %param.6) | copy-start | bytes 1769476
  51.8 1.0 copy-start
  51.9 1.4 copy-start.2
  51.9 1.9 %copy-start.4 = (bf16[256,16,128]{0,2,1:T(8,128)(2,1)}, bf16[256,16,128]{0,2,1:T(8,128)(2,1)S(1)}, u32[]{:S(2)}) copy-start(bf16[256,16,128]{0,2,1:T(8,128)(2,1)S(1)} %get-tuple-element.7) | copy-start | bytes 3145732
  51.9 2.3 %copy-start.6 = (bf16[256,16,128]{0,2,1:T(8,128)(2,1)}, bf16[256,16,128]{0,2,1:T(8,128)(2,1)S(1)}, u32[]{:S(2)}) copy-start(bf16[256,16,128]{0,2,1:T(8,128)(2,1)S(1)} %get-tuple-element.6) | copy-start | bytes 3145732
  51.9 2.7 %copy-start.8 = (bf16[256,16,128]{0,2,1:T(8,128)(2,1)}, bf16[256,16,128]{0,2,1:T(8,128)(2,1)S(1)}, u32[]{:S(2)}) copy-start(bf16[256,16,128]{0,2,1:T(8,128)(2,1)S(1)} %get-tuple-element.5) | copy-start | bytes 3145732
  51.9 3.2 %copy-start.10 = (bf16[256,16,128]{0,2,1:T(8,128)(2,1)}, bf16[256,16,128]{0,2,1:T(8,128)(2,1)S(1)}, u32[]{:S(2)}) copy-start(bf16[256,16,128]{0,2,1:T(8,128)(2,1)S(1)} %get-tuple-element.4) | copy-start | bytes 3145732
  51.9 3.6 %copy-start.11 = (bf16[256,16,128]{0,2,1:T(8,128)(2,1)}, bf16[256,16,128]{0,2,1:T(8,128)(2,1)S(1)}, u32[]{:S(2)}) copy-start(bf16[256,16,128]{0,2,1:T(8,128)(2,1)S(1)} %get-tuple-element.3) | copy-start | bytes 3145732
  55.1 1.2 copy-start.13
  55.1 1.2 copy-start.15
  57.1 5.5 %collective-permute-start.4 = (bf16[128,16,1]{0,2,1:T(2,128)(2,1)S(1)}, bf16[128,16,1]{0,2,1:T(2,128)(2,1)S(1)}, u32[]{:S(2)}, u32[]{:S(2)}) collective-permute-start(bf16[128,16,1]{0,2,1:T(2,128)(2,1)S(1)} %get-tuple-element.25), channel_id=1, source_target_pairs={{0,4},{4,8},{8,12},{12,0},{1,5},{5,9},{9,13},{13,1},{2,6},{6,10},{... | collective-permute-start | bytes 12296 | tf_op jit(solution)/shard_map/ppermute | solution.py:14
  58.6 4.0 %collective-permute-start.5 = (bf16[128,16,1]{0,2,1:T(2,128)(2,1)S(1)}, bf16[128,16,1]{0,2,1:T(2,128)(2,1)S(1)}, u32[]{:S(2)}, u32[]{:S(2)}) collective-permute-start(bf16[128,16,1]{0,2,1:T(2,128)(2,1)S(1)} %get-tuple-element.26), channel_id=1, source_target_pairs={{4,0},{8,4},{12,8},{0,12},{5,1},{9,5},{13,9},{1,13},{6,2},{10,6},{... | collective-permute-start | bytes 12296 | tf_op jit(solution)/shard_map/ppermute | solution.py:15
  62.6 1.3 collective-permute-start.6
  62.7 1.4 collective-permute-start.7
  73.4 95.1 %all-reduce.2.cloned.1.call-start = ((), (), s32[]{:S(2)}) async-start(), calls=%async_computation.3 | async-start | bytes 2359296 | tf_op jit(solution)/shard_map/psum | solution.py:69
  73.6 3.3 %copy-start.9 = (bf16[256,16,128]{0,2,1:T(8,128)(2,1)S(1)}, bf16[256,16,128]{0,2,1:T(8,128)(2,1)}, u32[]{:S(2)}) copy-start(bf16[256,16,128]{0,2,1:T(8,128)(2,1)} %copy-done.8) | copy-start | bytes 3145732
  75.3 2.1 %copy-start.7 = (bf16[256,16,128]{0,2,1:T(8,128)(2,1)S(1)}, bf16[256,16,128]{0,2,1:T(8,128)(2,1)}, u32[]{:S(2)}) copy-start(bf16[256,16,128]{0,2,1:T(8,128)(2,1)} %copy-done.6) | copy-start | bytes 3145732
  77.0 1.2 copy-start.5
  77.4 1.3 copy-start.3
  78.2 1.3 copy-start.1
Sparse Core Ops, SparseCore 0:
  18.3 25.1 all-gather.1
  73.5 32.3 reduce-scatter.1
  109.0 59.5 all-reduce.1
where the time goes:
time: 178 us; the launch traced here: 177 us
  waiting for transfers between devices  95.8 us (54%)
  local copies, waits for them, and re-layouts  19.5 us (11%)
  blocking collectives  17.9 us (10%)
  matrix products  15 us (8%)
  between operations  14.2 us (8%)
  starting transfers between devices  10.5 us (6%)
  other arithmetic  4.73 us (3%)
    psum x1, waiting for transfers between devices, local(): weight_grad, bias_grad = lax.psum((weight_part, bias_part), ('lon', 'lat'))  60.5 us
    all_gather x1, waiting for transfers between devices, local(): input_all = lax.all_gather(input_pad, 'chan', axis=0, tiled=True)  23.9 us
    psum x1, blocking collectives, local(): weight_grad, bias_grad = lax.psum((weight_part, bias_part), ('lon', 'lat'))  17.9 us
    slice x2, local copies, waits for them, and re-layouts, window_of(): field[:, first_row:first_row + row_count, first_col:first_col + column_co...  9.24 us
    reduce_scatter x1, waiting for transfers between devices, local(): lax.psum_scatter(summed.reshape(amount, row_count, column_count), 'chan',...  6.31 us
    unnamed x34, local copies, waits for them, and re-layouts  5.76 us
    dot_general x9, matrix products, local(): lax.dot_general(grad_pre, window, (((1,), (1,)), ((), ())), preferred_ele...  5.76 us
    ppermute x4, starting transfers between devices, padded_2(): after = lax.ppermute(initial, axis, down)  5.42 us
  transfers between devices with their start and end apart: 11, of which 9 were waited for; matrix products, arithmetic and copies ran while one was open for 6% of the time, Pallas kernels for 0%

commit v1 on v0

--- a/solution.py
+++ b/solution.py
@@ -42,7 +42,18 @@
 def local(inputs, cotangent, weight, bias_vector):
     own_channels, row_count, column_count = inputs.shape
     input_pad = mask_rims(padded_2(inputs, (("lon", 2), ("lat", 1)), 1))
-    input_all = lax.all_gather(input_pad, "chan", axis=0, tiled=True)
+    u1 = lax.axis_size("chan")
+    state_next, vec_out, base_arr = (u1, lax.axis_index("chan"), input_pad.shape[0])
+    mat_out, frame_out = (input_pad, 1)
+    while frame_out < state_next:
+        found = []
+        d = 0
+        while d < state_next:
+            found.append((d, (d - frame_out) % state_next))
+            d = d + 1
+        mat_out = jnp.concatenate([mat_out, lax.ppermute(mat_out, "chan", found)], axis=0)
+        frame_out = 2 * frame_out
+    input_all = jnp.roll(mat_out, vec_out * base_arr, axis=0)
     preact = jnp.zeros((own_channels, row_count * column_count), jnp.float32)
     for tap_row in range(3):
         for tap_col in range(3):

time: 178 us -> 140 us (0.79)
  waiting for transfers between devices: 95.8 us -> 59.4 us
  local copies, waits for them, and re-layouts: 19.5 us -> 13.6 us
    psum x1, waiting for transfers between devices: 60.5 us -> 34 us  [local(): weight_grad, bias_grad = lax.psum((weight_part, bias_part), ('lon', 'lat'))]
    all_gather x1 -> x0, waiting for transfers between devices: 23.9 us -> none  [local(): input_all = lax.all_gather(input_pad, 'chan', axis=0, tiled=True)]
    ppermute x0 -> x1, waiting for transfers between devices: none -> 13.3 us  [local(): lax.ppermute(mat_out, 'chan', found)]
    slice x2, local copies, waits for them, and re-layouts: 9.24 us -> 3.32 us  [window_of(): field[:, first_row:first_row + row_count, first_col:first_col + column_co...]
  transfers between devices with their start and end apart: 11 -> 11, of which waited for: 9 -> 9; matrix products, arithmetic and copies ran while one was open for 6% -> 7% of each run, Pallas kernels for 0% -> 0%
where the time goes in v1:
time: 140 us; the launch traced here: 139 us
  waiting for transfers between devices  59.4 us (42%)
  blocking collectives  18.2 us (13%)
  between operations  15.9 us (11%)
  matrix products  15 us (11%)
  local copies, waits for them, and re-layouts  13.6 us (10%)
  starting transfers between devices  12.2 us (9%)
  other arithmetic  4.95 us (4%)
    psum x1, waiting for transfers between devices, local(): weight_grad, bias_grad = lax.psum((weight_part, bias_part), ('lon', 'lat'))  34 us
    psum x1, blocking collectives, local(): weight_grad, bias_grad = lax.psum((weight_part, bias_part), ('lon', 'lat'))  18.2 us
    ppermute x1, waiting for transfers between devices, local(): lax.ppermute(mat_out, 'chan', found)  13.3 us
    reduce_scatter x1, waiting for transfers between devices, local(): lax.psum_scatter(summed.reshape(amount, row_count, column_count), 'chan',...  7.1 us
    unnamed x34, local copies, waits for them, and re-layouts  5.77 us
    dot_general x9, matrix products, local(): lax.dot_general(grad_pre, window, (((1,), (1,)), ((), ())), preferred_ele...  5.73 us
    ppermute x4, starting transfers between devices, padded_2(): after = lax.ppermute(initial, axis, down)  5.47 us
    dot_general x9, matrix products, local(): lax.dot_general(kernel_cols, window, (((0,), (0,)), ((), ())), preferred_...  5.08 us
  transfers between devices with their start and end apart: 11, of which 9 were waited for; matrix products, arithmetic and copies ran while one was open for 7% of the time, Pallas kernels for 0%

profile of v1, /device:TPU:0, one launch (start us, length us, event | category | flops | bytes accessed | tf_op | source)
XLA Modules:
  0.0 139.2 jit_solution(1489727267678419328)
XLA Ops:
  8.1 1.5 %copy.13 = bf16[128,16,128]{0,2,1:T(8,128)(2,1)S(1)} copy(bf16[128,16,128]{2,1,0:T(8,128)(2,1)} %param.4) | data formatting | bytes 1048576 | tf_op args[0]
  9.6 3.1 %collective-permute-start = (bf16[128,16,1]{0,2,1:T(2,128)(2,1)S(1)}, bf16[128,16,1]{0,2,1:T(2,128)(2,1)S(1)}, u32[]{:S(2)}, u32[]{:S(2)}) collective-permute-start(bf16[128,16,1]{0,2,1:T(2,128)(2,1)S(1)} %get-tuple-element.27), channel_id=1, source_target_pairs={{0,4},{4,8},{8,12},{12,0},{1,5},{5,9},{9,13},{13,1},{2,6},{6,10},{... | collective-permute-start | bytes 12296 | tf_op jit(solution)/shard_map/ppermute | solution.py:14
  12.7 2.1 %collective-permute-start.1 = (bf16[128,16,1]{0,2,1:T(2,128)(2,1)S(1)}, bf16[128,16,1]{0,2,1:T(2,128)(2,1)S(1)}, u32[]{:S(2)}, u32[]{:S(2)}) collective-permute-start(bf16[128,16,1]{0,2,1:T(2,128)(2,1)S(1)} %get-tuple-element.28), channel_id=1, source_target_pairs={{4,0},{8,4},{12,8},{0,12},{5,1},{9,5},{13,9},{1,13},{6,2},{10,6},{... | collective-permute-start | bytes 12296 | tf_op jit(solution)/shard_map/ppermute | solution.py:15
  14.8 1.6 %collective-permute-done = bf16[128,16,1]{0,2,1:T(2,128)(2,1)S(1)} collective-permute-done((bf16[128,16,1]{0,2,1:T(2,128)(2,1)S(1)}, bf16[128,16,1]{0,2,1:T(2,128)(2,1)S(1)}, u32[]{:S(2)}, u32[]{:S(2)}) %collective-permute-start) | collective-permute-done | bytes 4128 | tf_op jit(solution)/shard_map/ppermute | solution.py:14
  16.5 0.5 collective-permute-start.3
  17.0 0.7 collective-permute-done.2
  18.2 1.7 %collective-permute-start.4 = (bf16[128,18,130]{0,2,1:T(8,128)(2,1)S(1)}, bf16[128,18,130]{0,2,1:T(8,128)(2,1)S(1)}, u32[]{:S(2)}, u32[]{:S(2)}) collective-permute-start(bf16[128,18,130]{0,2,1:T(8,128)(2,1)S(1)} %maximum_select_fusion), channel_id=1, source_target_pairs={{0,2},{2,0},{1,3},{3,1},{4,6},{6,4},{5,7},{7,5},{8,10},{10,8},{9,1... | collective-permute-start | bytes 1797128 | tf_op jit(solution)/shard_map/ppermute | solution.py:54
  19.9 1.4 %copy.12 = f32[128,16,128]{0,2,1:T(8,128)} copy(bf16[128,16,128]{2,1,0:T(8,128)(2,1)S(1)} %copy-done.14) | data formatting | bytes 1572864 | tf_op jit(solution)/shard_map/convert_element_type | solution.py:65
  21.3 13.3 %collective-permute-done.4 = bf16[128,18,130]{0,2,1:T(8,128)(2,1)S(1)} collective-permute-done((bf16[128,18,130]{0,2,1:T(8,128)(2,1)S(1)}, bf16[128,18,130]{0,2,1:T(8,128)(2,1)S(1)}, u32[]{:S(2)}, u32[]{:S(2)}) %collective-permute-start.4) | collective-permute-done | bytes 599072 | tf_op jit(solution)/shard_map/ppermute | solution.py:54
  34.6 1.0 fusion.4
  35.6 2.4 %fusion.49 = (bf16[256,16,128]{0,2,1:T(8,128)(2,1)S(1)}, bf16[256,16,128]{0,2,1:T(8,128)(2,1)S(1)}, bf16[256,16,128]{0,2,1:T(8,128)(2,1)S(1)}, bf16[256,16,128]{...) fusion(bf16[256,18,130]{0,2,1:T(8,128)(2,1)S(1)} %fusion.4), kind=kLoop, calls=%fused_computation.93 | loop fusion | bytes 18874368 | tf_op jit(solution)/shard_map/slice | solution.py:37
  38.6 0.4 convolution_add_fusion.15
  41.7 0.8 copy-done.13
  42.5 0.7 convert_reduce_fusion
  43.3 1.5 %collective-permute-start.5 = (bf16[128,16,1]{0,2,1:T(2,128)(2,1)S(1)}, bf16[128,16,1]{0,2,1:T(2,128)(2,1)S(1)}, u32[]{:S(2)}, u32[]{:S(2)}) collective-permute-start(bf16[128,16,1]{0,2,1:T(2,128)(2,1)S(1)} %get-tuple-element.25), channel_id=1, source_target_pairs={{0,4},{4,8},{8,12},{12,0},{1,5},{5,9},{9,13},{13,1},{2,6},{6,10},{... | collective-permute-start | bytes 12296 | tf_op jit(solution)/shard_map/ppermute | solution.py:14
  44.8 2.4 %collective-permute-start.6 = (bf16[128,16,1]{0,2,1:T(2,128)(2,1)S(1)}, bf16[128,16,1]{0,2,1:T(2,128)(2,1)S(1)}, u32[]{:S(2)}, u32[]{:S(2)}) collective-permute-start(bf16[128,16,1]{0,2,1:T(2,128)(2,1)S(1)} %get-tuple-element.26), channel_id=1, source_target_pairs={{4,0},{8,4},{12,8},{0,12},{5,1},{9,5},{13,9},{1,13},{6,2},{10,6},{... | collective-permute-start | bytes 12296 | tf_op jit(solution)/shard_map/ppermute | solution.py:15
  47.2 1.6 %collective-permute-done.5 = bf16[128,16,1]{0,2,1:T(2,128)(2,1)S(1)} collective-permute-done((bf16[128,16,1]{0,2,1:T(2,128)(2,1)S(1)}, bf16[128,16,1]{0,2,1:T(2,128)(2,1)S(1)}, u32[]{:S(2)}, u32[]{:S(2)}) %collective-permute-start.5) | collective-permute-done | bytes 4128 | tf_op jit(solution)/shard_map/ppermute | solution.py:14
  48.9 0.5 collective-permute-start.8
  49.4 0.7 collective-permute-done.7
  50.6 0.9 fusion.50
  54.9 1.7 %convolution_add_fusion = f32[2048,256]{1,0:T(8,128)} fusion(f32[2048,256]{1,0:T(8,128)S(1)} %convolution_add_fusion.1, bf16[128,2048]{0,1:T(8,128)(2,1)S(1)} %bitcast.157, bf16[3,3,128,256]{3,2,1,0:T(8,128)(2,1)S(1)} %copy-done.12), kind=kOutput, calls=%fused_computation | convolution fusion | flops 134742016 | bytes 4784128 | tf_op jit(solution)/shard_map/dot_general | solution.py:89
  56.6 3.0 %copy.16 = f32[256,16,128]{2,1,0:T(8,128)} copy(f32[256,16,128]{0,2,1:T(8,128)} %bitcast.154) | data formatting | bytes 4194304 | tf_op jit(solution)/shard_map/reshape | solution.py:93
  59.9 1.7 %convolution_bitcast_fusion = f32[1,128,256]{2,1,0:T(8,128)S(1)} fusion(bf16[128,2048]{0,1:T(8,128)(2,1)S(1)} %get-tuple-element.30, bf16[256,2048]{0,1:T(8,128)(2,1)} %bitcast.156), kind=kOutput, calls=%fused_computation.27 | convolution fusion | flops 134217728 | bytes 1703936 | tf_op jit(solution)/shard_map/dot_general | solution.py:74
  61.6 1.7 %convolution_bitcast_fusion.1 = f32[1,128,256]{2,1,0:T(8,128)S(1)} fusion(bf16[128,2048]{0,1:T(8,128)(2,1)S(1)} %get-tuple-element.30, bf16[256,2048]{0,1:T(8,128)(2,1)} %bitcast.153), kind=kOutput, calls=%fused_computation.28 | convolution fusion | flops 134217728 | bytes 1703936 | tf_op jit(solution)/shard_map/dot_general | solution.py:74
  64.0 0.4 copy-done.5
  65.3 0.5 copy-done.1
  66.9 1.1 pad_maximum_fusion
  68.0 18.2 %psum.15 = f32[128]{0:T(128)} all-reduce(f32[128]{0:T(128)S(1)} %get-tuple-element.29), channel_id=1, replica_groups=mesh['groups'=2,'lon'=4,'chan'=2,'lat'=2] {'lon','lat'}, use_global_device_ids=true, to_apply=%region_3.4 | all-reduce | flops 128 | bytes 1024 | tf_op jit(solution)/shard_map/psum | solution.py:80
  86.2 7.1 %reduce-scatter.2.cloned.1.call-done = f32[128,16,128]{2,1,0:T(8,128)} async-done(((f32[256,16,128]{2,1,0:T(8,128)}), f32[128,16,128]{2,1,0:T(8,128)}) %reduce-scatter.2.cloned.1.call-update) | async-done | bytes 1048592 | tf_op jit(solution)/shard_map/reduce_scatter | solution.py:92
  93.3 2.1 %convert_element_type.18 = bf16[128,16,128]{2,1,0:T(8,128)(2,1)} convert(f32[128,16,128]{2,1,0:T(8,128)} %reduce-scatter.2.cloned.1.call-done) | non-fusion elementwise | flops 262144 | bytes 1572864 | tf_op jit(solution)/shard_map/convert_element_type | solution.py:95
  95.4 34.0 %all-reduce.2.cloned.1.call-done = f32[3,3,128,256]{3,2,1,0:T(8,128)} async-done(((f32[3,3,128,256]{3,2,1,0:T(8,128)}), f32[3,3,128,256]{3,2,1,0:T(8,128)}) %all-reduce.2.cloned.1.call-update) | async-done | bytes 1179664 | tf_op jit(solution)/shard_map/psum | solution.py:80
  129.4 2.4 %copy.18 = f32[3,3,128,256]{3,2,1,0:T(8,128)} copy(f32[3,3,128,256]{3,2,1,0:T(8,128)} %all-reduce.2.cloned.1.call-done) | data formatting | bytes 2359296
  (70 shorter events, 10.6 us)
Async XLA Ops:
  8.0 11.9 %copy-start.14 = (bf16[128,16,128]{2,1,0:T(8,128)(2,1)S(1)}, bf16[128,16,128]{2,1,0:T(8,128)(2,1)}, u32[]{:S(2)}) copy-start(bf16[128,16,128]{2,1,0:T(8,128)(2,1)} %param.5) | copy-start | bytes 1572868
  8.0 85.3 %reduce-scatter.2.cloned.1.call-start = ((), (), s32[]{:S(2)}) async-start(), calls=%async_computation.1 | async-start | bytes 3145728 | tf_op jit(solution)/shard_map/reduce_scatter | solution.py:92
  9.6 6.8 %collective-permute-start = (bf16[128,16,1]{0,2,1:T(2,128)(2,1)S(1)}, bf16[128,16,1]{0,2,1:T(2,128)(2,1)S(1)}, u32[]{:S(2)}, u32[]{:S(2)}) collective-permute-start(bf16[128,16,1]{0,2,1:T(2,128)(2,1)S(1)} %get-tuple-element.27), channel_id=1, source_target_pairs={{0,4},{4,8},{8,12},{12,0},{1,5},{5,9},{9,13},{13,1},{2,6},{6,10},{... | collective-permute-start | bytes 12296 | tf_op jit(solution)/shard_map/ppermute | solution.py:14
  12.7 3.7 %collective-permute-start.1 = (bf16[128,16,1]{0,2,1:T(2,128)(2,1)S(1)}, bf16[128,16,1]{0,2,1:T(2,128)(2,1)S(1)}, u32[]{:S(2)}, u32[]{:S(2)}) collective-permute-start(bf16[128,16,1]{0,2,1:T(2,128)(2,1)S(1)} %get-tuple-element.28), channel_id=1, source_target_pairs={{4,0},{8,4},{12,8},{0,12},{5,1},{9,5},{13,9},{1,13},{6,2},{10,6},{... | collective-permute-start | bytes 12296 | tf_op jit(solution)/shard_map/ppermute | solution.py:15
  16.4 1.3 collective-permute-start.2
  16.5 1.4 collective-permute-start.3
  18.2 16.4 %collective-permute-start.4 = (bf16[128,18,130]{0,2,1:T(8,128)(2,1)S(1)}, bf16[128,18,130]{0,2,1:T(8,128)(2,1)S(1)}, u32[]{:S(2)}, u32[]{:S(2)}) collective-permute-start(bf16[128,18,130]{0,2,1:T(8,128)(2,1)S(1)} %maximum_select_fusion), channel_id=1, source_target_pairs={{0,2},{2,0},{1,3},{3,1},{4,6},{6,4},{5,7},{7,5},{8,10},{10,8},{9,1... | collective-permute-start | bytes 1797128 | tf_op jit(solution)/shard_map/ppermute | solution.py:54
  35.6 2.5 %copy-start.12 = (bf16[3,3,128,256]{3,2,1,0:T(8,128)(2,1)S(1)}, bf16[3,3,128,256]{3,2,1,0:T(8,128)(2,1)}, u32[]{:S(2)}) copy-start(bf16[3,3,128,256]{3,2,1,0:T(8,128)(2,1)} %param.6) | copy-start | bytes 1769476
  38.1 1.0 copy-start
  38.1 1.4 %copy-start.2 = (bf16[256,16,128]{0,2,1:T(8,128)(2,1)}, bf16[256,16,128]{0,2,1:T(8,128)(2,1)S(1)}, u32[]{:S(2)}) copy-start(bf16[256,16,128]{0,2,1:T(8,128)(2,1)S(1)} %get-tuple-element.8) | copy-start | bytes 3145732
  38.1 1.9 %copy-start.4 = (bf16[256,16,128]{0,2,1:T(8,128)(2,1)}, bf16[256,16,128]{0,2,1:T(8,128)(2,1)S(1)}, u32[]{:S(2)}) copy-start(bf16[256,16,128]{0,2,1:T(8,128)(2,1)S(1)} %get-tuple-element.7) | copy-start | bytes 3145732
  38.1 2.3 %copy-start.6 = (bf16[256,16,128]{0,2,1:T(8,128)(2,1)}, bf16[256,16,128]{0,2,1:T(8,128)(2,1)S(1)}, u32[]{:S(2)}) copy-start(bf16[256,16,128]{0,2,1:T(8,128)(2,1)S(1)} %get-tuple-element.6) | copy-start | bytes 3145732
  38.1 2.7 %copy-start.8 = (bf16[256,16,128]{0,2,1:T(8,128)(2,1)}, bf16[256,16,128]{0,2,1:T(8,128)(2,1)S(1)}, u32[]{:S(2)}) copy-start(bf16[256,16,128]{0,2,1:T(8,128)(2,1)S(1)} %get-tuple-element.5) | copy-start | bytes 3145732
  38.1 3.2 %copy-start.10 = (bf16[256,16,128]{0,2,1:T(8,128)(2,1)}, bf16[256,16,128]{0,2,1:T(8,128)(2,1)S(1)}, u32[]{:S(2)}) copy-start(bf16[256,16,128]{0,2,1:T(8,128)(2,1)S(1)} %get-tuple-element.4) | copy-start | bytes 3145732
  38.1 3.6 %copy-start.11 = (bf16[256,16,128]{0,2,1:T(8,128)(2,1)}, bf16[256,16,128]{0,2,1:T(8,128)(2,1)S(1)}, u32[]{:S(2)}) copy-start(bf16[256,16,128]{0,2,1:T(8,128)(2,1)S(1)} %get-tuple-element.3) | copy-start | bytes 3145732
  41.3 1.2 copy-start.13
  41.3 1.2 copy-start.15
  43.3 5.5 %collective-permute-start.5 = (bf16[128,16,1]{0,2,1:T(2,128)(2,1)S(1)}, bf16[128,16,1]{0,2,1:T(2,128)(2,1)S(1)}, u32[]{:S(2)}, u32[]{:S(2)}) collective-permute-start(bf16[128,16,1]{0,2,1:T(2,128)(2,1)S(1)} %get-tuple-element.25), channel_id=1, source_target_pairs={{0,4},{4,8},{8,12},{12,0},{1,5},{5,9},{9,13},{13,1},{2,6},{6,10},{... | collective-permute-start | bytes 12296 | tf_op jit(solution)/shard_map/ppermute | solution.py:14
  44.8 4.0 %collective-permute-start.6 = (bf16[128,16,1]{0,2,1:T(2,128)(2,1)S(1)}, bf16[128,16,1]{0,2,1:T(2,128)(2,1)S(1)}, u32[]{:S(2)}, u32[]{:S(2)}) collective-permute-start(bf16[128,16,1]{0,2,1:T(2,128)(2,1)S(1)} %get-tuple-element.26), channel_id=1, source_target_pairs={{4,0},{8,4},{12,8},{0,12},{5,1},{9,5},{13,9},{1,13},{6,2},{10,6},{... | collective-permute-start | bytes 12296 | tf_op jit(solution)/shard_map/ppermute | solution.py:15
  48.8 1.3 collective-permute-start.7
  48.9 1.4 collective-permute-start.8
  59.7 69.7 %all-reduce.2.cloned.1.call-start = ((), (), s32[]{:S(2)}) async-start(), calls=%async_computation.2 | async-start | bytes 2359296 | tf_op jit(solution)/shard_map/psum | solution.py:80
  59.9 3.3 %copy-start.9 = (bf16[256,16,128]{0,2,1:T(8,128)(2,1)S(1)}, bf16[256,16,128]{0,2,1:T(8,128)(2,1)}, u32[]{:S(2)}) copy-start(bf16[256,16,128]{0,2,1:T(8,128)(2,1)} %copy-done.8) | copy-start | bytes 3145732
  61.6 2.1 %copy-start.7 = (bf16[256,16,128]{0,2,1:T(8,128)(2,1)S(1)}, bf16[256,16,128]{0,2,1:T(8,128)(2,1)}, u32[]{:S(2)}) copy-start(bf16[256,16,128]{0,2,1:T(8,128)(2,1)} %copy-done.6) | copy-start | bytes 3145732
  63.2 1.2 copy-start.5
  63.6 1.3 copy-start.3
  64.5 1.3 copy-start.1
Sparse Core Ops, SparseCore 0:
  59.8 33.4 reduce-scatter.1
Sparse Core Ops, SparseCore 1:
  68.1 61.2 all-reduce.1
